TPU v7x, 512 devices: a whole 4x8x8 slice. The times are simulated.
512 devices in a mesh: grp: 8 (over z_hi, core), req: 64 (over y, x, z_lo).
Axes of the slice: x: 4, y: 8, z: 8 (z_hi: 4, z_lo: 2; z = z_hi * 2 + z_lo), core: 2. Of those that a mesh axis runs over, the one named last changes fastest.
Arguments:
- queries: bfloat16 [8, 64, 4, 2048], P('grp', 'req'), may hold values from -12 to 1700
- suffix_kv: bfloat16 [8, 64, 2, 4, 512], P('grp', 'req'), may hold values from -6 to 6
- prefix_pool: bfloat16 [8, 64, 3, 2, 128, 512], P('grp', 'req'), may hold values from -6 to 6
- page_table: int32 [64, 16], P('req'), may hold values from 0 to 23, as said below
- suffix_len: int32 [8, 64], P('grp'), may hold values from 1 to 4, 128 in all within a row
- residual: bfloat16 [8, 256, 4096], P('grp', None, 'req'), may hold values from -40 to 40
- out_weight: bfloat16 [2048, 4096], P(None, 'req'), may hold values from -0.5 to 0.5
- norm_gain: bfloat16 [4096], P('req'), may hold values from 0.099609375 to 1.8984375
- gate_up: bfloat16 [2, 4096, 8192], P(None, None, 'req'), may hold values from -0.09375 to 0.09375
- down_weight: bfloat16 [8192, 4096], P('req'), may hold values from -0.1875 to 0.1875
Outputs:
- hidden_out: bfloat16 [8, 256, 4096], P('grp', None, 'req')
Inputs may be any that keep to these rules, and one draw needn't show every extreme that they name: `page_table`: row b lists 16 different pages of group b's pool; pool page p is slot p % 3 on the member p // 3.
All inputs are finite; a program needn't handle non-finite values.
Results may differ from a plain program's by a relative error of at most 0.028.
Values may be sent and summed in bfloat16 or wider, within the bound.
No kernel may reach another device: no remote copies, remote signals or barrier semaphores. Data moves between devices by JAX's collectives and lax.ppermute only.
A program may use at most 64 MiB of HBM per device.

v0:
```python
import jax
import jax.numpy as jnp
from jax import lax
from jax.sharding import PartitionSpec as P

D = 4096
HD = 128
QH = 16
KVH = 4
PAGE = 128


def split_heads(query_rows):
    row_count = query_rows.shape[0]
    query_heads = query_rows.reshape(row_count, KVH, QH // KVH, HD)
    return jnp.transpose(query_heads, (1, 2, 0, 3))


def empty_state(row_count):
    running_max = jnp.full((KVH, QH // KVH, row_count), -1e30, jnp.float32)
    weight_sum = jnp.zeros((KVH, QH // KVH, row_count), jnp.float32)
    accumulated = jnp.zeros((KVH, QH // KVH, row_count, HD), jnp.float32)
    return (running_max, weight_sum, accumulated)


def page_block(softmax_state, pages_part, query_heads, table_row):
    running_max, weight_sum, accumulated = softmax_state
    page_count = pages_part.shape[0]
    page_index = jnp.arange(page_count, dtype=jnp.int32)
    page_used = jnp.any(page_index[:, None] == table_row[None, :], axis=1)
    token_live = jnp.repeat(page_used, PAGE)
    key_rows = pages_part[:, 0].reshape(page_count * PAGE, KVH, HD)
    value_rows = pages_part[:, 1].reshape(page_count * PAGE, KVH, HD)
    scores = jnp.einsum(
        "jgsd,tjd->jgst", query_heads, key_rows, preferred_element_type=jnp.float32
    ) * HD ** (-0.5)
    scores = jnp.where(token_live, scores, -1e30)
    merged_max = jnp.maximum(running_max, jnp.max(scores, axis=-1))
    weights = jnp.where(token_live, jnp.exp(scores - merged_max[..., None]), 0.0)
    weight_sum = jnp.sum(weights, axis=-1)
    weighted = jnp.einsum(
        "jgst,tjd->jgsd",
        weights.astype(jnp.bfloat16),
        value_rows,
        preferred_element_type=jnp.float32,
    )
    accumulated = weighted
    return (merged_max, weight_sum, accumulated)


def with_suffix(softmax_state, query_heads, own_suffix):
    running_max, weight_sum, accumulated = softmax_state
    row_count = query_heads.shape[2]
    key_rows = own_suffix[0].reshape(row_count, KVH, HD)
    value_rows = own_suffix[1].reshape(row_count, KVH, HD)
    scores = jnp.einsum(
        "jgsd,tjd->jgst", query_heads, key_rows, preferred_element_type=jnp.float32
    ) * HD ** (-0.5)
    causal = jnp.arange(row_count)[:, None] >= jnp.arange(row_count)[None, :]
    scores = jnp.where(causal, scores, -1e30)
    merged_max = jnp.maximum(running_max, jnp.max(scores, axis=-1))
    weights = jnp.where(causal, jnp.exp(scores - merged_max[..., None]), 0.0)
    rescale = jnp.exp(running_max - merged_max)
    weight_sum = weight_sum * rescale + jnp.sum(weights, axis=-1)
    weighted = jnp.einsum(
        "jgst,tjd->jgsd",
        weights.astype(jnp.bfloat16),
        value_rows,
        preferred_element_type=jnp.float32,
    )
    accumulated = accumulated * rescale[..., None] + weighted
    accumulated = accumulated / weight_sum[..., None]
    ordered = jnp.transpose(accumulated, (2, 0, 1, 3))
    return ordered.reshape(row_count, QH * HD).astype(jnp.bfloat16)


def body(
    queries,
    suffix_kv,
    prefix_pool,
    page_table,
    suffix_len,
    residual,
    out_weight,
    norm_gain,
    gate_up,
    down_weight,
):
    slot_count = queries.shape[2]
    own_queries = queries[0, 0]
    own_pool = prefix_pool[0, 0]
    table_row = page_table[0]
    own_heads = split_heads(own_queries)
    softmax_state = page_block(
        empty_state(slot_count),
        lax.all_gather(own_pool, "grp", axis=0, tiled=True),
        own_heads,
        table_row,
    )
    attention = with_suffix(softmax_state, own_heads, suffix_kv[0, 0])
    projected = jnp.dot(
        lax.all_gather(attention, "req", axis=0, tiled=True),
        out_weight,
        preferred_element_type=jnp.float32,
    )
    stream = (residual[0].astype(jnp.float32) + projected).astype(jnp.bfloat16)
    wide_local = stream.astype(jnp.float32)
    partial_sq = jnp.sum(wide_local * wide_local, axis=1)
    row_sumsq = lax.psum(partial_sq, "req")
    inverse_rms = lax.rsqrt(row_sumsq / D + 1e-05)
    normed = (wide_local * inverse_rms[:, None] * norm_gain.astype(jnp.float32)[None, :]).astype(
        jnp.bfloat16
    )
    gate_up_out = jnp.einsum(
        "nc,kcf->knf",
        lax.all_gather(normed, "req", axis=1, tiled=True),
        gate_up,
        preferred_element_type=jnp.float32,
    )
    hidden = (jax.nn.silu(gate_up_out[0]) * gate_up_out[1]).astype(jnp.bfloat16)
    partial_value = jnp.dot(hidden, down_weight, preferred_element_type=jnp.float32)
    summed = lax.psum_scatter(partial_value, "req", scatter_dimension=1, tiled=True)
    lengths = suffix_len[0]
    slot_index = jnp.arange(stream.shape[0], dtype=jnp.int32) % slot_count
    slot_live = (slot_index < jnp.repeat(lengths, slot_count)).astype(jnp.float32)
    result_rows = (wide_local + summed) * slot_live[:, None]
    return result_rows.astype(jnp.bfloat16)[None]


def solution(mesh):
    return jax.shard_map(
        body,
        mesh=mesh,
        in_specs=(
            P("grp", "req", None, None),
            P("grp", "req", None, None, None),
            P("grp", "req", None, None, None, None),
            P("req", None),
            P("grp", None),
            P("grp", None, "req"),
            P(None, "req"),
            P("req"),
            P(None, None, "req"),
            P("req", None),
        ),
        out_specs=P("grp", None, "req"),
        check_vma=False,
    )
```

profile of v0, /device:TPU:128, one launch (start us, length us, event | category | flops | bytes accessed | tf_op | source)
XLA Modules:
  0.0 1206.9 jit_solution(9325458423505003093)
XLA Ops:
  6.5 0.0 copy-start
  6.5 0.0 all-gather.8.cloned.1.call-start
  6.5 0.7 all-gather.8.cloned.1.call-update
  7.3 0.0 all-gather.10.cloned.1.call-start
  7.3 0.7 fusion.46
  8.1 0.1 broadcast_bitcast_fusion
  8.1 1.0 fusion.58
  9.1 76.7 %all-gather.8.cloned.1.call-done = bf16[1,1,24,2,128,512]{5,4,3,1,0,2:T(8,128)(2,1)} async-done(((bf16[1,1,3,2,128,512]{5,4,3,1,0,2:T(8,128)(2,1)}), bf16[1,1,24,2,128,512]{5,4,3,1,0,2:T(8,128)(2,1)}) %all-gather.8.cloned.1.call-update) | async-done | bytes 6291472 | tf_op jit(solution)/shard_map/all_gather | solution.py:96
  85.8 6.2 fusion.56
  92.0 0.0 copy-start.5
  92.0 5.5 reshape.67
  97.5 0.0 copy-start.6
  97.5 0.0 copy-done.5
  97.5 2.9 fusion.57
  100.5 0.0 copy-done.6
  100.5 0.2 convolution_bitcast_fusion
  100.7 5.5 reshape.68
  106.2 0.0 copy-start.7
  106.2 0.5 fusion.27
  106.7 0.0 copy-start.2
  106.8 0.0 copy-start.3
  106.8 3.4 fusion.24
  110.2 0.0 all-gather.10.cloned.1.call-update
  110.2 0.0 all-gather.6.cloned.1.call-start
  110.2 0.0 copy-done.7
  110.3 299.2 %all-gather.10.cloned.1.call-done = bf16[64,4,2048]{2,1,0:T(4,128)(2,1)} async-done(((bf16[1,4,2048]{2,1,0:T(4,128)(2,1)}), bf16[64,4,2048]{2,1,0:T(4,128)(2,1)}) %all-gather.10.cloned.1.call-update) | async-done | bytes 1048592 | tf_op jit(solution)/shard_map/all_gather | solution.py:102
  409.4 1.3 reshape.60
  410.8 0.0 copy-done.2
  410.8 0.0 copy-done.3
  410.8 0.5 multiply_reduce_fusion
  411.3 156.7 %psum.7 = f32[256]{0:T(256)S(1)} all-reduce(f32[256]{0:T(256)S(1)} %get-tuple-element.15), channel_id=1, replica_groups=mesh['grp'=8,'req'=64] {'req'}, use_global_device_ids=true, to_apply=%region_6.7 | all-reduce | flops 256 | bytes 2048 | tf_op jit(solution)/shard_map/psum | solution.py:109
  568.0 0.7 multiply_convert_fusion.1
  568.7 0.0 all-gather.6.cloned.1.call-update
  568.7 0.0 copy-start.1
  568.7 0.0 reduce-scatter.2.cloned.1.call-start
  568.7 298.6 %all-gather.6.cloned.1.call-done = bf16[256,4096]{0,1:T(8,128)(2,1)} async-done(((bf16[256,64]{0,1:T(8,128)(2,1)}), bf16[256,4096]{0,1:T(8,128)(2,1)}) %all-gather.6.cloned.1.call-update) | async-done | bytes 2097168 | tf_op jit(solution)/shard_map/all_gather | solution.py:116
  867.4 0.0 copy-done
  867.4 2.3 fusion.6
  869.7 0.0 copy-done.1
  869.7 2.7 fusion.35
  872.4 0.0 copy-start.4
  872.4 0.0 reduce-scatter.2.cloned.1.call-update
  872.4 0.6 copy-done.4
  873.1 0.1 broadcast_in_dim.56
  873.1 0.1 reshape.56
  873.3 325.7 %reduce-scatter.2.cloned.1.call-done = f32[256,64]{0,1:T(8,128)} async-done(((f32[256,4096]{0,1:T(8,128)}), f32[256,64]{0,1:T(8,128)}) %reduce-scatter.2.cloned.1.call-update) | async-done | bytes 65552 | tf_op jit(solution)/shard_map/reduce_scatter | solution.py:122
  1199.0 1.5 fusion.38
  (7 shorter events, 0.1 us)
Async XLA Ops:
  6.5 860.8 %copy-start = (bf16[2,4096,128]{2,1,0:T(8,128)(2,1)S(1)}, bf16[2,4096,128]{2,1,0:T(8,128)(2,1)}, u32[]{:S(2)}) copy-start(bf16[2,4096,128]{2,1,0:T(8,128)(2,1)} %param.18) | copy-start | bytes 6291460
  6.5 79.3 %all-gather.8.cloned.1.call-start = ((), (), s32[]{:S(2)}) async-start(), calls=%async_computation.3 | async-start | bytes 7077888 | tf_op jit(solution)/shard_map/all_gather | solution.py:96
  7.3 402.2 %all-gather.10.cloned.1.call-start = ((), (), s32[]{:S(2)}) async-start(), calls=%async_computation.4 | async-start | bytes 1064960 | tf_op jit(solution)/shard_map/all_gather | solution.py:102
  92.0 5.5 copy-start.5
  97.5 3.0 copy-start.6
  106.2 4.0 copy-start.7
  106.7 304.1 %copy-start.2 = (bf16[2048,64]{0,1:T(8,128)(2,1)S(1)}, bf16[2048,64]{0,1:T(8,128)(2,1)}, u32[]{:S(2)}) copy-start(bf16[2048,64]{0,1:T(8,128)(2,1)} %param.16) | copy-start | bytes 786436
  106.8 304.1 %copy-start.3 = (bf16[1,256,64]{1,2,0:T(8,128)(2,1)S(1)}, bf16[1,256,64]{1,2,0:T(8,128)(2,1)}, u32[]{:S(2)}) copy-start(bf16[1,256,64]{1,2,0:T(8,128)(2,1)} %param.15) | copy-start | bytes 98308
  110.2 757.2 %all-gather.6.cloned.1.call-start = ((), (), s32[]{:S(2)}) async-start(), calls=%async_computation.1 | async-start | bytes 2129920 | tf_op jit(solution)/shard_map/all_gather | solution.py:116
  568.7 301.0 %copy-start.1 = (bf16[128,4096]{1,0:T(8,128)(2,1)S(1)}, bf16[128,4096]{1,0:T(8,128)(2,1)}, u32[]{:S(2)}) copy-start(bf16[128,4096]{1,0:T(8,128)(2,1)} %param.19) | copy-start | bytes 3145732
  568.7 630.3 %reduce-scatter.2.cloned.1.call-start = ((), (), s32[]{:S(2)}) async-start(), calls=%async_computation.2 | async-start | bytes 4259840 | tf_op jit(solution)/shard_map/reduce_scatter | solution.py:122
  872.4 0.7 copy-start.4
Sparse Core Ops, SparseCore 0:
  9.5 76.3 all-gather.7
  110.3 299.0 all-gather.9
  568.8 298.5 all-gather.5
  872.6 326.3 reduce-scatter.1
where the time goes:
time: 1210 us
  waiting for transfers between devices  1000 us (83%)
  blocking collectives  157 us (13%)
  local copies, waits for them, and re-layouts  19.5 us (2%)
  between operations  13.3 us (1%)
  matrix products  13 us (1%)
    reduce_scatter x1, waiting for transfers between devices, body(): lax.psum_scatter(partial_value, 'req', scatter_dimension=1, tiled=True)  326 us
    all_gather x1, waiting for transfers between devices, body(): lax.all_gather(attention, 'req', axis=0, tiled=True)  299 us
    all_gather x1, waiting for transfers between devices, body(): lax.all_gather(normed, 'req', axis=1, tiled=True)  299 us
    psum x1, blocking collectives, body(): row_sumsq = lax.psum(partial_sq, 'req')  157 us
    all_gather x1, waiting for transfers between devices, body(): lax.all_gather(own_pool, 'grp', axis=0, tiled=True)  76.7 us
  transfers between devices with their start and end apart: 4, of which 4 were waited for; matrix products, arithmetic and copies ran while one was open for 0% of the time, Pallas kernels for 0%

commit v1 on v0

--- a/solution.py
+++ b/solution.py
@@ -93,7 +93,9 @@
     own_heads = split_heads(own_queries)
     softmax_state = page_block(
         empty_state(slot_count),
-        lax.all_gather(own_pool, "grp", axis=0, tiled=True),
+        jnp.concatenate(
+            lax.all_to_all(jnp.stack([own_pool] * lax.axis_size("grp")), "grp", 0, 0), axis=0
+        ),
         own_heads,
         table_row,
     )

time: 1210 us -> 1280 us (1.058)
  waiting for transfers between devices: 1000 us -> 1060 us
    all_to_all x0 -> x1, waiting for transfers between devices: none -> 118 us  [body(): lax.all_to_all(jnp.stack([own_pool] * lax.axis_size('grp')), 'grp', 0, 0)]
    all_gather x1 -> x0, waiting for transfers between devices: 76.7 us -> none  [body(): lax.all_gather(own_pool, 'grp', axis=0, tiled=True)]
    all_gather x1, waiting for transfers between devices: 299 us -> 321 us  [body(): lax.all_gather(attention, 'req', axis=0, tiled=True)]
where the time goes in v1:
time: 1280 us
  waiting for transfers between devices  1060 us (83%)
  blocking collectives  157 us (12%)
  local copies, waits for them, and re-layouts  24.2 us (2%)
  between operations  13.2 us (1%)
    reduce_scatter x1, waiting for transfers between devices, body(): lax.psum_scatter(partial_value, 'req', scatter_dimension=1, tiled=True)  325 us
    all_gather x1, waiting for transfers between devices, body(): lax.all_gather(attention, 'req', axis=0, tiled=True)  321 us
    all_gather x1, waiting for transfers between devices, body(): lax.all_gather(normed, 'req', axis=1, tiled=True)  299 us
    psum x1, blocking collectives, body(): row_sumsq = lax.psum(partial_sq, 'req')  157 us
    all_to_all x1, waiting for transfers between devices, body(): lax.all_to_all(jnp.stack([own_pool] * lax.axis_size('grp')), 'grp', 0, 0)  118 us
  transfers between devices with their start and end apart: 4, of which 4 were waited for; matrix products, arithmetic and copies ran while one was open for 0% of the time, Pallas kernels for 0%

profile of v1, /device:TPU:128, one launch (start us, length us, event | category | flops | bytes accessed | tf_op | source)
XLA Modules:
  0.0 1281.1 jit_solution(2650842302263137617)
XLA Ops:
  6.5 0.0 copy-start
  6.5 4.7 stack.3
  11.2 0.0 copy-start.7
  11.2 0.0 copy-start.5
  11.2 0.0 copy-start.6
  11.2 9.2 all-to-all-start
  20.4 0.0 all-gather.6.cloned.1.call-start
  20.4 0.0 copy-done.7
  20.4 0.1 fusion.46
  20.5 0.1 broadcast_bitcast_fusion
  20.6 0.0 copy-done.5
  20.6 0.0 copy-done.6
  20.6 0.3 fusion.58
  20.9 117.6 %all-to-all-done = bf16[8,3,2,128,512]{4,3,2,1,0:T(8,128)(2,1)} async-done(((bf16[8,3,2,128,512]{4,3,2,1,0:T(8,128)(2,1)}), bf16[8,3,2,128,512]{4,3,2,1,0:T(8,128)(2,1)}, u32[]{:S(2)}, u32[]{:S(2)}) %all-to-all-start) | async-done | bytes 6291488 | tf_op jit(solution)/shard_map/all_to_all | solution.py:97
  138.4 6.2 fusion.56
  144.7 5.5 reshape.72
  150.2 2.9 fusion.57
  153.1 0.2 convolution_bitcast_fusion
  153.3 5.5 reshape.73
  158.8 0.0 copy-start.8
  158.8 0.5 fusion.27
  159.3 0.0 copy-start.2
  159.4 0.0 copy-start.3
  159.4 3.4 fusion.24
  162.8 0.0 all-gather.6.cloned.1.call-update
  162.8 0.0 all-gather.4.cloned.1.call-start
  162.8 0.0 copy-done.8
  162.9 320.9 %all-gather.6.cloned.1.call-done = bf16[64,4,2048]{2,1,0:T(4,128)(2,1)} async-done(((bf16[1,4,2048]{2,1,0:T(4,128)(2,1)}), bf16[64,4,2048]{2,1,0:T(4,128)(2,1)}) %all-gather.6.cloned.1.call-update) | async-done | bytes 1048592 | tf_op jit(solution)/shard_map/all_gather | solution.py:104
  483.8 1.3 reshape.65
  485.1 0.0 copy-done.2
  485.1 0.0 copy-done.3
  485.1 0.5 multiply_reduce_fusion
  485.6 156.7 %psum.7 = f32[256]{0:T(256)S(1)} all-reduce(f32[256]{0:T(256)S(1)} %get-tuple-element.15), channel_id=1, replica_groups=mesh['grp'=8,'req'=64] {'req'}, use_global_device_ids=true, to_apply=%region_6.7 | all-reduce | flops 256 | bytes 2048 | tf_op jit(solution)/shard_map/psum | solution.py:111
  642.3 0.7 multiply_convert_fusion.1
  643.0 0.0 all-gather.4.cloned.1.call-update
  643.0 0.0 copy-start.1
  643.0 0.0 reduce-scatter.2.cloned.1.call-start
  643.1 298.6 %all-gather.4.cloned.1.call-done = bf16[256,4096]{0,1:T(8,128)(2,1)} async-done(((bf16[256,64]{0,1:T(8,128)(2,1)}), bf16[256,4096]{0,1:T(8,128)(2,1)}) %all-gather.4.cloned.1.call-update) | async-done | bytes 2097168 | tf_op jit(solution)/shard_map/all_gather | solution.py:118
  941.7 0.0 copy-done
  941.7 2.3 fusion.6
  944.0 0.0 copy-done.1
  944.0 2.7 fusion.35
  946.7 0.0 reduce-scatter.2.cloned.1.call-update
  946.8 0.6 copy-done.4
  947.4 0.1 broadcast_in_dim.56
  947.5 0.1 reshape.62
  947.6 325.5 %reduce-scatter.2.cloned.1.call-done = f32[256,64]{0,1:T(8,128)} async-done(((f32[256,4096]{0,1:T(8,128)}), f32[256,64]{0,1:T(8,128)}) %reduce-scatter.2.cloned.1.call-update) | async-done | bytes 65552 | tf_op jit(solution)/shard_map/reduce_scatter | solution.py:124
  1273.1 1.5 fusion.38
  (8 shorter events, 0.1 us)
Async XLA Ops:
  6.5 935.2 %copy-start = (bf16[2,4096,128]{2,1,0:T(8,128)(2,1)S(1)}, bf16[2,4096,128]{2,1,0:T(8,128)(2,1)}, u32[]{:S(2)}) copy-start(bf16[2,4096,128]{2,1,0:T(8,128)(2,1)} %param.18) | copy-start | bytes 6291460
  11.2 9.2 copy-start.7
  11.2 9.4 copy-start.5
  11.2 9.4 copy-start.6
  11.2 127.2 %all-to-all-start = ((bf16[8,3,2,128,512]{4,3,2,1,0:T(8,128)(2,1)}), bf16[8,3,2,128,512]{4,3,2,1,0:T(8,128)(2,1)}, u32[]{:S(2)}, u32[]{:S(2)}) async-start(bf16[8,3,2,128,512]{4,3,2,1,0:T(8,128)(2,1)} %stack.3), calls=%async_computation | async-start | bytes 12582912 | tf_op jit(solution)/shard_map/all_to_all | solution.py:97
  20.4 463.4 %all-gather.6.cloned.1.call-start = ((), (), s32[]{:S(2)}) async-start(), calls=%async_computation.4 | async-start | bytes 1064960 | tf_op jit(solution)/shard_map/all_gather | solution.py:104
  158.8 4.0 copy-start.8
  159.3 325.8 %copy-start.2 = (bf16[2048,64]{0,1:T(8,128)(2,1)S(1)}, bf16[2048,64]{0,1:T(8,128)(2,1)}, u32[]{:S(2)}) copy-start(bf16[2048,64]{0,1:T(8,128)(2,1)} %param.16) | copy-start | bytes 786436
  159.4 325.8 %copy-start.3 = (bf16[1,256,64]{1,2,0:T(8,128)(2,1)S(1)}, bf16[1,256,64]{1,2,0:T(8,128)(2,1)}, u32[]{:S(2)}) copy-start(bf16[1,256,64]{1,2,0:T(8,128)(2,1)} %param.15) | copy-start | bytes 98308
  162.8 778.9 %all-gather.4.cloned.1.call-start = ((), (), s32[]{:S(2)}) async-start(), calls=%async_computation.2 | async-start | bytes 2129920 | tf_op jit(solution)/shard_map/all_gather | solution.py:118
  643.0 301.0 %copy-start.1 = (bf16[128,4096]{1,0:T(8,128)(2,1)S(1)}, bf16[128,4096]{1,0:T(8,128)(2,1)}, u32[]{:S(2)}) copy-start(bf16[128,4096]{1,0:T(8,128)(2,1)} %param.19) | copy-start | bytes 3145732
  643.0 630.1 %reduce-scatter.2.cloned.1.call-start = ((), (), s32[]{:S(2)}) async-start(), calls=%async_computation.3 | async-start | bytes 4259840 | tf_op jit(solution)/shard_map/reduce_scatter | solution.py:124
  946.7 0.7 copy-start.4
Sparse Core Ops, SparseCore 0:
  162.9 320.8 all-gather.5
  643.1 298.5 all-gather.3
  946.9 326.1 reduce-scatter.1
